TPU v7x, 256 devices: a whole 4x4x8 slice. The times are simulated.
256 devices in a mesh: band: 16 (over x, y_hi, core), req: 16 (over y_lo, z).
Axes of the slice: x: 4, y: 4 (y_hi: 2, y_lo: 2; y = y_hi * 2 + y_lo), z: 8, core: 2. Of those that a mesh axis runs over, the one named last changes fastest.
Arguments:
- latents: bfloat16 [16, 64, 512, 320], P('req', 'band'), may hold values from -40 to 40
- request_time_embedding: bfloat16 [16, 1280], P('req'), may hold values from -6 to 6
- request_adapter: int32 [16, 1], P('req'), may hold values from 0 to 255, as said below
- adapter_stored_row: int32 [256], replicated, may hold values from 0 to 255, as said below
- first_conv_weight: bfloat16 [3, 3, 320, 320], replicated, may hold values from -0.109375 to 0.109375
- stored_down_weight: bfloat16 [256, 3, 3, 320, 64], P(('band', 'req')), may hold values from -0.109375 to 0.109375
- stored_up_weight: bfloat16 [256, 64, 320], P(('band', 'req')), may hold values from -0.75 to 0.75
- second_conv_weight: bfloat16 [3, 3, 320, 320], replicated, may hold values from -0.109375 to 0.109375
- time_projection_weight: bfloat16 [1280, 320], replicated, may hold values from -0.15625 to 0.15625
Outputs:
- block_out: bfloat16 [16, 64, 512, 320], P('req', 'band')
Inputs may be any that keep to these rules, and one draw needn't show every extreme that they name: `request_adapter`: ids of adapters. `adapter_stored_row`: each stored row appears once.
All inputs are finite; a program needn't handle non-finite values.
Results may differ from a plain program's by a relative error of at most 0.0038.
Values may be sent and summed in bfloat16 or wider, within the bound.
No kernel may reach another device: no remote copies, remote signals or barrier semaphores. Data moves between devices by JAX's collectives and lax.ppermute only.
A program may use at most 128 MiB of HBM per device.

v0:
```python
import jax
import jax.numpy as jnp
from jax import lax
from jax.sharding import PartitionSpec as P

G = 32


def with_halo(x, sides, width):
    for axis, dim in sides:
        count, length = (lax.axis_size(axis), x.shape[dim])
        up = [(i, (i + 1) % count) for i in range(count - 1)]
        down = [(j, i) for i, j in up]
        last = lax.slice_in_dim(x, length - width, length, axis=dim)
        initial = lax.slice_in_dim(x, 0, width, axis=dim)
        before = lax.ppermute(last, axis, up)
        after = lax.ppermute(initial, axis, down)
        x = jnp.concatenate([before, x, after], axis=dim)
    return x


def group_norm(field, groups, total_rows):
    requests, rows, width, channels = field.shape
    grouped = field.reshape(requests, rows, width, groups, channels // groups)
    count = total_rows * width * (channels // groups)
    sums = lax.psum(jnp.sum(grouped, axis=(1, 2, 4)), "band")
    center = (sums / count)[:, None, None, :, None]
    deviation = grouped - center
    spread = lax.psum(jnp.sum(deviation * deviation, axis=(1, 2, 4)), "band") / count
    normed = deviation * lax.rsqrt(spread + 1e-05)[:, None, None, :, None]
    return normed.reshape(field.shape)


def padded_field(field):
    extended = with_halo(field, (("band", 1),), 1)
    return jnp.pad(extended, ((0, 0), (0, 0), (1, 1), (0, 0)))


def convolve(padded, kernel, rows, width):
    total = None
    for row_tap in range(3):
        for col_tap in range(3):
            term = jnp.einsum(
                "qhwc,cd->qhwd",
                padded[:, row_tap : row_tap + rows, col_tap : col_tap + width],
                kernel[row_tap, col_tap],
                preferred_element_type=jnp.float32,
            )
            total = term if total is None else total + term
    return total


def convolve_each(padded, kernels, rows, width):
    total = None
    for row_tap in range(3):
        for col_tap in range(3):
            term = jnp.einsum(
                "qhwc,qcd->qhwd",
                padded[:, row_tap : row_tap + rows, col_tap : col_tap + width],
                kernels[:, row_tap, col_tap],
                preferred_element_type=jnp.float32,
            )
            total = term if total is None else total + term
    return total


def select_rows(slots, to_global, pieces):
    down_piece, up_piece = pieces
    count = down_piece.shape[0]
    stored = to_global(jnp.arange(count, dtype=jnp.int32))
    matches = stored[None, :] == slots[:, None]
    zero = jnp.zeros((), down_piece.dtype)
    down_pick = jnp.sum(
        jnp.where(matches[:, :, None, None, None, None], down_piece[None], zero), axis=1
    )
    up_pick = jnp.sum(jnp.where(matches[:, :, None, None], up_piece[None], zero), axis=1)
    return (down_pick, up_pick)


def slots_of(adapter_ids, adapter_stored_row):
    adapter_count = adapter_stored_row.shape[0]
    picked = adapter_ids == jnp.arange(adapter_count, dtype=jnp.int32)[None, :]
    return jnp.sum(jnp.where(picked, adapter_stored_row[None, :], 0), axis=1)


def shards(
    latents,
    request_time_embedding,
    request_adapter,
    adapter_stored_row,
    first_conv_weight,
    stored_down_weight,
    stored_up_weight,
    second_conv_weight,
    time_projection_weight,
):
    requests, rows, width, channels = latents.shape
    total_rows = rows * lax.axis_size("band")
    held_adapters = stored_down_weight.shape[0]
    req_count = lax.axis_size("req")
    slots = slots_of(request_adapter, adapter_stored_row)
    band_base = lax.axis_index("band") * (req_count * held_adapters)

    def column_global(gathered):
        return band_base + gathered

    part_down, part_up = select_rows(
        slots,
        column_global,
        (
            lax.all_gather(stored_down_weight, "req", axis=0, tiled=True),
            lax.all_gather(stored_up_weight, "req", axis=0, tiled=True),
        ),
    )
    sum_down, sum_up = (
        lax.psum(part_down, "band").astype(jnp.float32),
        lax.psum(part_up, "band").astype(jnp.float32),
    )
    chosen_down = sum_down.astype(jnp.bfloat16)
    chosen_up = sum_up.astype(jnp.bfloat16)
    shift = jnp.dot(
        jax.nn.silu(request_time_embedding.astype(jnp.float32)).astype(jnp.bfloat16),
        time_projection_weight,
        preferred_element_type=jnp.float32,
    )
    groups = G
    first = jax.nn.silu(group_norm(latents.astype(jnp.float32), groups, total_rows)).astype(
        jnp.bfloat16
    )
    first_padded = padded_field(first)
    main = convolve(first_padded, first_conv_weight, rows, width)
    lowrank = convolve_each(first_padded, chosen_down, rows, width).astype(jnp.bfloat16)
    lifted = jnp.einsum("qhwk,qkc->qhwc", lowrank, chosen_up, preferred_element_type=jnp.float32)
    hidden = main + lifted + shift[:, None, None, :]
    second = jax.nn.silu(group_norm(hidden, groups, total_rows)).astype(jnp.bfloat16)
    result = latents.astype(jnp.float32) + convolve(
        padded_field(second), second_conv_weight, rows, width
    )
    return result.astype(jnp.bfloat16)


def solution(mesh):
    in_specs = (
        P("req", "band", None, None),
        P("req", None),
        P("req", None),
        P(),
        P(),
        P(("band", "req"), None, None, None, None),
        P(("band", "req"), None, None),
        P(),
        P(),
    )
    out_specs = P("req", "band", None, None)
    return jax.shard_map(shards, mesh=mesh, in_specs=in_specs, out_specs=out_specs, check_vma=False)
```

profile of v0, /device:TPU:1, one launch (start us, length us, event | category | flops | bytes accessed | tf_op | source)
XLA Modules:
  0.0 536.1 jit_solution(17608430378172255338)
XLA Ops:
  6.5 0.7 all-gather.2.cloned.1.call-update
  7.3 1.6 convert_reduce_fusion
  9.1 93.4 %psum.42 = f32[1,32]{1,0:T(1,128)S(1)} all-reduce(f32[1,32]{1,0:T(1,128)S(1)} %bitcast.261), channel_id=1, replica_groups=mesh['band'=16,'req'=16] {'band'}, use_global_device_ids=true, to_apply=%region_2.3 | all-reduce | flops 32 | bytes 256 | tf_op jit(solution)/shard_map/psum | solution.py:26
  103.5 33.5 %psum.43 = f32[1,32]{1,0:T(1,128)S(1)} all-reduce(f32[1,32]{1,0:T(1,128)S(1)} %bitcast.262), channel_id=1, replica_groups=mesh['band'=16,'req'=16] {'band'}, use_global_device_ids=true, to_apply=%region_5.6 | all-reduce | flops 32 | bytes 256 | tf_op jit(solution)/shard_map/psum | solution.py:29
  137.2 1.0 fusion.8
  138.2 2.1 collective-permute-start
  140.3 4.1 collective-permute-start.1
  145.1 0.7 fusion.108
  145.7 0.6 add_compare_fusion
  146.7 28.0 %all_gather.7 = bf16[16,64,320]{2,1,0:T(8,128)(2,1)S(1)} all-gather(bf16[1,64,320]{2,1,0:T(8,128)(2,1)S(1)} %copy-done.13), channel_id=1, replica_groups=mesh['band'=16,'req'=16] {'req'}, dimensions={0}, use_global_device_ids=true | all-gather | bytes 696320 | tf_op jit(solution)/shard_map/all_gather | solution.py:112
  174.9 3.4 fusion.32
  178.3 64.7 %psum.45 = bf16[64,320]{1,0:T(8,128)(2,1)S(1)} all-reduce(bf16[64,320]{1,0:T(8,128)(2,1)S(1)} %select_reduce_fusion.1), channel_id=1, replica_groups=mesh['band'=16,'req'=16] {'band'}, use_global_device_ids=true, to_apply=%region_10.11 | all-reduce | flops 20480 | bytes 81920 | tf_op jit(solution)/shard_map/psum | solution.py:117
  243.0 3.4 fusion.56
  246.4 3.2 fusion.15
  249.7 2.5 fusion.54
  252.2 2.4 fusion.52
  254.6 2.5 fusion.51
  257.1 2.4 fusion.49
  259.4 2.5 fusion.47
  262.0 6.3 %select_reduce_fusion = bf16[3,3,320,64]{2,3,1,0:T(8,128)(2,1)} fusion(bf16[16,3,3,320,64]{3,4,2,1,0:T(8,128)(2,1)} %all-gather.2.cloned.1.call-done, pred[16]{0:T(512)(128)(4,1)S(1)} %add_compare_fusion), kind=kLoop, calls=%fused_computation.2 | loop fusion | flops 5713920 | bytes 6266896 | tf_op jit(solution)/shard_map/reduce_sum | solution.py:73
  268.3 3.8 fusion.60
  272.1 3.3 fusion.41
  275.4 132.5 %all-reduce.4.cloned.1.call-done = bf16[1,3,3,320,64]{3,4,2,1,0:T(8,128)(2,1)} async-done(((bf16[1,3,3,320,64]{3,4,2,1,0:T(8,128)(2,1)}), bf16[1,3,3,320,64]{3,4,2,1,0:T(8,128)(2,1)}) %all-reduce.4.cloned.1.call-update) | async-done | bytes 368656 | tf_op jit(solution)/shard_map/psum | solution.py:116
  407.9 1.8 fusion.34
  409.8 2.5 fusion.62
  413.4 0.6 fusion.48
  414.0 1.4 fusion.55
  415.4 1.2 fusion.46
  416.6 13.4 %fusion.118 = (f32[320]{0:T(512)S(1)}, f32[4,512,320]{1,2,0:T(8,128)}) fusion(f32[320]{0:T(512)S(1)} %convolution_reduce_fusion, bf16[64,320]{1,0:T(8,128)(2,1)S(1)} %psum.45, f32[4,512,64]{1,2,0:T(8,128)} %fusion.55, f32[4,512,64]{1,2,0:T(8,128)} %fusion.62, f32[4,512,64]{1,2,0:T(8,128)S(1)} %fusion.53, f32[4,512,64]{1,2,0:T(8,128)} %fusion.46, ...), kind=kOutput, calls=%fused_computation.158 | convolution fusion | flops 175636160 | bytes 29723904 | tf_op jit(solution)/shard_map/qhwk,qkc->qhwc/dot_general | solution.py:133
  430.2 33.8 %psum.46 = f32[1,32]{1,0:T(1,128)S(1)} all-reduce(f32[1,32]{1,0:T(1,128)S(1)} %bitcast.263), channel_id=1, replica_groups=mesh['band'=16,'req'=16] {'band'}, use_global_device_ids=true, to_apply=%region_13.14 | all-reduce | flops 32 | bytes 256 | tf_op jit(solution)/shard_map/psum | solution.py:26
  464.1 2.2 multiply_reduce_fusion
  466.5 36.5 %psum.47 = f32[1,32]{1,0:T(1,128)S(1)} all-reduce(f32[1,32]{1,0:T(1,128)S(1)} %bitcast.260), channel_id=1, replica_groups=mesh['band'=16,'req'=16] {'band'}, use_global_device_ids=true, to_apply=%region_16.17 | all-reduce | flops 32 | bytes 256 | tf_op jit(solution)/shard_map/psum | solution.py:29
  503.2 0.9 fusion.121
  504.2 1.9 collective-permute-start.2
  506.1 2.4 collective-permute-start.3
  508.6 2.8 fusion.68
  511.4 2.3 collective-permute-done.2
  513.6 2.4 collective-permute-done.3
  516.0 1.7 select_maximum_fusion
  517.7 0.9 fusion.21
  518.6 1.0 fusion.22
  519.6 0.9 fusion.23
  520.5 1.0 fusion.24
  521.6 0.9 fusion.29
  522.4 0.9 fusion.26
  523.3 0.9 fusion.18
  524.6 0.8 copy-done.9
  525.5 3.8 fusion.10
  (65 shorter events, 4.4 us)
Async XLA Ops:
  6.5 139.8 %copy-start = (bf16[1280,320]{0,1:T(8,128)(2,1)S(1)}, bf16[1280,320]{0,1:T(8,128)(2,1)}, u32[]{:S(2)}) copy-start(bf16[1280,320]{0,1:T(8,128)(2,1)} %param.17) | copy-start | bytes 2457604
  6.5 96.2 %copy-start.5 = (bf16[1,4,512,320]{2,3,1,0:T(8,128)(2,1)S(1)}, bf16[1,4,512,320]{2,3,1,0:T(8,128)(2,1)}, u32[]{:S(2)}) copy-start(bf16[1,4,512,320]{2,3,1,0:T(8,128)(2,1)} %param.9) | copy-start | bytes 3932164
  6.5 255.4 %all-gather.2.cloned.1.call-start = ((), (), s32[]{:S(2)}) async-start(), calls=%async_computation | async-start | bytes 7520256 | tf_op jit(solution)/shard_map/all_gather | solution.py:111
  7.3 400.7 %all-reduce.4.cloned.1.call-start = ((), (), s32[]{:S(2)}) async-start(), calls=%async_computation.1 | async-start | bytes 884736 | tf_op jit(solution)/shard_map/psum | solution.py:116
  102.7 42.3 %copy-start.15 = (s32[256]{0:T(256)S(1)}, s32[256]{0:T(256)}, u32[]{:S(2)}) copy-start(s32[256]{0:T(256)} %param.12) | copy-start | bytes 3076
  102.7 43.6 %copy-start.14 = (bf16[1,1280]{1,0:T(2,128)(2,1)S(1)}, bf16[1,1280]{1,0:T(2,128)(2,1)}, u32[]{:S(2)}) copy-start(bf16[1,1280]{1,0:T(2,128)(2,1)} %param.10) | copy-start | bytes 7684
  103.3 43.5 %copy-start.13 = (bf16[1,64,320]{2,1,0:T(8,128)(2,1)S(1)}, bf16[1,64,320]{2,1,0:T(8,128)(2,1)}, u32[]{:S(2)}) copy-start(bf16[1,64,320]{2,1,0:T(8,128)(2,1)} %param.15) | copy-start | bytes 122884
  138.1 104.9 %copy-start.2 = (bf16[1,4,512,320]{2,3,1,0:T(8,128)(2,1)}, bf16[1,4,512,320]{2,3,1,0:T(8,128)(2,1)S(1)}, u32[]{:S(2)}) copy-start(bf16[1,4,512,320]{2,3,1,0:T(8,128)(2,1)S(1)} %fusion.8) | copy-start | bytes 3932164
  138.2 104.8 %collective-permute-start = (bf16[1,1,512,320]{2,3,1,0:T(8,128)(2,1)S(1)}, bf16[1,1,512,320]{2,3,1,0:T(8,128)(2,1)S(1)}, u32[]{:S(2)}, u32[]{:S(2)}) collective-permute-start(bf16[1,1,512,320]{2,3,1,0:T(8,128)(2,1)S(1)} %get-tuple-element.7), channel_id=1, source_target_pairs={{0,16},{16,32},{32,48},{48,64},{64,80},{80,96},{96,112},{112,128},... | collective-permute-start | bytes 983048 | tf_op jit(solution)/shard_map/ppermute | solution.py:16
  140.3 106.1 %collective-permute-start.1 = (bf16[1,1,512,320]{2,3,1,0:T(8,128)(2,1)S(1)}, bf16[1,1,512,320]{2,3,1,0:T(8,128)(2,1)}, u32[]{:S(2)}, u32[]{:S(2)}) collective-permute-start(bf16[1,1,512,320]{2,3,1,0:T(8,128)(2,1)S(1)} %get-tuple-element.8), channel_id=1, source_target_pairs={{16,0},{32,16},{48,32},{64,48},{80,64},{96,80},{112,96},{128,112},... | collective-permute-start | bytes 983048 | tf_op jit(solution)/shard_map/ppermute | solution.py:17
  243.0 3.4 copy-start.7
  246.4 3.3 copy-start.10
  275.4 136.9 %copy-start.8 = (bf16[1,1,512,320]{2,3,1,0:T(8,128)(2,1)S(1)}, bf16[1,1,512,320]{2,3,1,0:T(8,128)(2,1)}, u32[]{:S(2)}) copy-start(bf16[1,1,512,320]{2,3,1,0:T(8,128)(2,1)} %copy-done.7) | copy-start | bytes 983044
  407.9 4.4 copy-start.3
  407.9 4.4 copy-start.12
  429.9 73.2 %copy-start.4 = (f32[4,512,320]{1,2,0:T(8,128)S(1)}, f32[4,512,320]{1,2,0:T(8,128)}, u32[]{:S(2)}) copy-start(f32[4,512,320]{1,2,0:T(8,128)} %get-tuple-element.10) | copy-start | bytes 7864324
  503.2 5.4 %copy-start.11 = (bf16[3,3,320,320]{3,2,1,0:T(8,128)(2,1)S(1)}, bf16[3,3,320,320]{3,2,1,0:T(8,128)(2,1)}, u32[]{:S(2)}) copy-start(bf16[3,3,320,320]{3,2,1,0:T(8,128)(2,1)} %param.16) | copy-start | bytes 5529604
  504.2 9.4 %collective-permute-start.2 = (bf16[1,1,512,320]{2,3,1,0:T(8,128)(2,1)S(1)}, bf16[1,1,512,320]{2,3,1,0:T(8,128)(2,1)S(1)}, u32[]{:S(2)}, u32[]{:S(2)}) collective-permute-start(bf16[1,1,512,320]{2,3,1,0:T(8,128)(2,1)S(1)} %get-tuple-element.5), channel_id=1, source_target_pairs={{0,16},{16,32},{32,48},{48,64},{64,80},{80,96},{96,112},{112,128},... | collective-permute-start | bytes 983048 | tf_op jit(solution)/shard_map/ppermute | solution.py:16
  506.1 9.9 %collective-permute-start.3 = (bf16[1,1,512,320]{2,3,1,0:T(8,128)(2,1)S(1)}, bf16[1,1,512,320]{2,3,1,0:T(8,128)(2,1)S(1)}, u32[]{:S(2)}, u32[]{:S(2)}) collective-permute-start(bf16[1,1,512,320]{2,3,1,0:T(8,128)(2,1)S(1)} %get-tuple-element.6), channel_id=1, source_target_pairs={{16,0},{32,16},{48,32},{64,48},{80,64},{96,80},{112,96},{128,112},... | collective-permute-start | bytes 983048 | tf_op jit(solution)/shard_map/ppermute | solution.py:17
  523.3 1.3 copy-start.6
  523.3 2.1 copy-start.9
  525.4 3.8 copy-start.1
Sparse Core Ops, SparseCore 0:
  9.1 91.5 all-gather.1
  268.4 139.4 all-reduce.3
where the time goes:
time: 537 us; the launch traced here: 536 us
  blocking collectives  290 us (54%)
  waiting for transfers between devices  138 us (26%)
  matrix products  61.5 us (11%)
  other arithmetic  19.3 us (4%)
  between operations  14.4 us (3%)
  starting transfers between devices  10.6 us (2%)
    psum x1, waiting for transfers between devices, shards(): lax.psum(part_down, 'band').astype(jnp.float32)  133 us
    psum x2, blocking collectives, group_norm(): sums = lax.psum(jnp.sum(grouped, axis=(1, 2, 4)), 'band')  127 us
    psum x2, blocking collectives, group_norm(): lax.psum(jnp.sum(deviation * deviation, axis=(1, 2, 4)), 'band') / count  70 us
    psum x1, blocking collectives, shards(): lax.psum(part_up, 'band').astype(jnp.float32)  64.7 us
    dot_general x18, matrix products, convolve(): jnp.einsum('qhwc,cd->qhwd', padded[:, row_tap:row_tap + rows, col_tap:col...  39.2 us
    all_gather x1, blocking collectives, shards(): lax.all_gather(stored_up_weight, 'req', axis=0, tiled=True)  28 us
    dot_general x1, matrix products, shards(): jnp.einsum('qhwk,qkc->qhwc', lowrank, chosen_up, preferred_element_type=j...  13.4 us
  transfers between devices with their start and end apart: 6, of which 3 were waited for; matrix products, arithmetic and copies ran while one was open for 7% of the time, Pallas kernels for 0%

commit v1 on v0

--- a/solution.py
+++ b/solution.py
@@ -109,7 +109,10 @@
         column_global,
         (
             lax.all_gather(stored_down_weight, "req", axis=0, tiled=True),
-            lax.all_gather(stored_up_weight, "req", axis=0, tiled=True),
+            jnp.concatenate(
+                lax.all_to_all(jnp.stack([stored_up_weight] * lax.axis_size("req")), "req", 0, 0),
+                axis=0,
+            ),
         ),
     )
     sum_down, sum_up = (

time: 537 us -> 452 us (0.84)
  waiting for transfers between devices: 138 us -> 73.5 us
  blocking collectives: 290 us -> 258 us
  starting transfers between devices: 10.6 us -> 21.2 us
    psum x1, waiting for transfers between devices: 133 us -> 68.3 us  [shards(): lax.psum(part_down, 'band').astype(jnp.float32)]
    all_gather x1 -> x0, blocking collectives: 28 us -> none  [shards(): lax.all_gather(stored_up_weight, 'req', axis=0, tiled=True)]
    all_to_all x0 -> x1, starting transfers between devices: none -> 10.2 us  [shards(): lax.all_to_all(jnp.stack([stored_up_weight] * lax.axis_size('req')), 'req...]
  transfers between devices with their start and end apart: 6 -> 7, of which waited for: 3 -> 3; matrix products, arithmetic and copies ran while one was open for 7% -> 10% of each run, Pallas kernels for 0% -> 0%
where the time goes in v1:
time: 452 us; the launch traced here: 451 us
  blocking collectives  258 us (57%)
  waiting for transfers between devices  73.5 us (16%)
  matrix products  59.4 us (13%)
  starting transfers between devices  21.2 us (5%)
  other arithmetic  18.9 us (4%)
  between operations  14.4 us (3%)
  local copies, waits for them, and re-layouts  5.07 us (1%)
    psum x2, blocking collectives, group_norm(): sums = lax.psum(jnp.sum(grouped, axis=(1, 2, 4)), 'band')  128 us
    psum x2, blocking collectives, group_norm(): lax.psum(jnp.sum(deviation * deviation, axis=(1, 2, 4)), 'band') / count  70.1 us
    psum x1, waiting for transfers between devices, shards(): lax.psum(part_down, 'band').astype(jnp.float32)  68.3 us
    psum x1, blocking collectives, shards(): lax.psum(part_up, 'band').astype(jnp.float32)  60.1 us
    dot_general x18, matrix products, convolve(): jnp.einsum('qhwc,cd->qhwd', padded[:, row_tap:row_tap + rows, col_tap:col...  37.3 us
    dot_general x1, matrix products, shards(): jnp.einsum('qhwk,qkc->qhwc', lowrank, chosen_up, preferred_element_type=j...  13.2 us
    all_to_all x1, starting transfers between devices, shards(): lax.all_to_all(jnp.stack([stored_up_weight] * lax.axis_size('req')), 'req...  10.2 us
  transfers between devices with their start and end apart: 7, of which 3 were waited for; matrix products, arithmetic and copies ran while one was open for 10% of the time, Pallas kernels for 0%

profile of v1, /device:TPU:1, one launch (start us, length us, event | category | flops | bytes accessed | tf_op | source)
XLA Modules:
  0.0 450.9 jit_solution(9425658248556156179)
XLA Ops:
  6.5 0.7 all-gather.2.cloned.1.call-update
  7.3 1.8 stack.2
  9.0 10.2 %all-to-all-start = ((bf16[16,1,64,320]{3,2,1,0:T(8,128)(2,1)}), bf16[16,1,64,320]{3,2,1,0:T(8,128)(2,1)}, u32[]{:S(2)}, u32[]{:S(2)}) async-start(bf16[16,1,64,320]{3,2,1,0:T(8,128)(2,1)} %stack.2), calls=%async_computation | async-start | bytes 1572864 | tf_op jit(solution)/shard_map/all_to_all | solution.py:113
  19.8 94.5 %psum.42 = f32[1,32]{1,0:T(1,128)S(1)} all-reduce(f32[1,32]{1,0:T(1,128)S(1)} %bitcast.267), channel_id=1, replica_groups=mesh['band'=16,'req'=16] {'band'}, use_global_device_ids=true, to_apply=%region_2.3 | all-reduce | flops 32 | bytes 256 | tf_op jit(solution)/shard_map/psum | solution.py:26
  115.2 33.6 %psum.43 = f32[1,32]{1,0:T(1,128)S(1)} all-reduce(f32[1,32]{1,0:T(1,128)S(1)} %bitcast.268), channel_id=1, replica_groups=mesh['band'=16,'req'=16] {'band'}, use_global_device_ids=true, to_apply=%region_5.6 | all-reduce | flops 32 | bytes 256 | tf_op jit(solution)/shard_map/psum | solution.py:29
  149.0 1.0 fusion.8
  150.0 2.2 collective-permute-start
  152.2 4.2 collective-permute-start.1
  157.1 0.7 fusion.109
  158.9 3.4 fusion.32
  162.3 0.7 copy-done.8
  163.0 2.9 fusion.15
  166.0 2.6 fusion.54
  168.5 2.3 fusion.52
  170.9 2.6 fusion.51
  173.4 2.3 fusion.49
  175.8 2.5 fusion.47
  178.3 2.4 fusion.41
  180.7 2.4 fusion.57
  183.0 6.3 %select_reduce_fusion = bf16[3,3,320,64]{2,3,1,0:T(8,128)(2,1)} fusion(bf16[16,3,3,320,64]{3,4,2,1,0:T(8,128)(2,1)} %all-gather.2.cloned.1.call-done, pred[16]{0:T(512)(128)(4,1)S(1)} %add_compare_fusion), kind=kLoop, calls=%fused_computation.2 | loop fusion | flops 5713920 | bytes 6266896 | tf_op jit(solution)/shard_map/reduce_sum | solution.py:73
  189.3 3.8 fusion.61
  193.2 1.3 fusion.56
  194.5 60.1 %psum.45 = bf16[64,320]{1,0:T(8,128)(2,1)S(1)} all-reduce(bf16[64,320]{1,0:T(8,128)(2,1)S(1)} %fusion.56), channel_id=1, replica_groups=mesh['band'=16,'req'=16] {'band'}, use_global_device_ids=true, to_apply=%region_10.11 | all-reduce | flops 20480 | bytes 81920 | tf_op jit(solution)/shard_map/psum | solution.py:120
  254.6 68.3 %all-reduce.4.cloned.1.call-done = bf16[1,3,3,320,64]{3,4,2,1,0:T(8,128)(2,1)} async-done(((bf16[1,3,3,320,64]{3,4,2,1,0:T(8,128)(2,1)}), bf16[1,3,3,320,64]{3,4,2,1,0:T(8,128)(2,1)}) %all-reduce.4.cloned.1.call-update) | async-done | bytes 368656 | tf_op jit(solution)/shard_map/psum | solution.py:119
  322.9 1.8 fusion.34
  324.8 2.5 fusion.63
  329.0 1.4 fusion.55
  330.4 1.2 fusion.46
  331.6 13.2 %fusion.119 = (f32[320]{0:T(512)S(1)}, f32[4,512,320]{1,2,0:T(8,128)}) fusion(f32[320]{0:T(512)S(1)} %convolution_reduce_fusion, bf16[64,320]{1,0:T(8,128)(2,1)S(1)} %psum.45, f32[4,512,64]{1,2,0:T(8,128)} %fusion.55, f32[4,512,64]{1,2,0:T(8,128)} %fusion.63, f32[4,512,64]{1,2,0:T(8,128)S(1)} %fusion.53, f32[4,512,64]{1,2,0:T(8,128)} %fusion.46, ...), kind=kOutput, calls=%fused_computation.159 | convolution fusion | flops 175636160 | bytes 29723904 | tf_op jit(solution)/shard_map/qhwk,qkc->qhwc/dot_general | solution.py:136
  345.0 33.8 %psum.46 = f32[1,32]{1,0:T(1,128)S(1)} all-reduce(f32[1,32]{1,0:T(1,128)S(1)} %bitcast.269), channel_id=1, replica_groups=mesh['band'=16,'req'=16] {'band'}, use_global_device_ids=true, to_apply=%region_13.14 | all-reduce | flops 32 | bytes 256 | tf_op jit(solution)/shard_map/psum | solution.py:26
  378.9 2.2 multiply_reduce_fusion
  381.3 36.5 %psum.47 = f32[1,32]{1,0:T(1,128)S(1)} all-reduce(f32[1,32]{1,0:T(1,128)S(1)} %bitcast.266), channel_id=1, replica_groups=mesh['band'=16,'req'=16] {'band'}, use_global_device_ids=true, to_apply=%region_16.17 | all-reduce | flops 32 | bytes 256 | tf_op jit(solution)/shard_map/psum | solution.py:29
  418.0 0.9 fusion.122
  419.0 1.9 collective-permute-start.2
  420.9 2.7 collective-permute-start.3
  423.6 2.8 fusion.69
  426.4 2.0 collective-permute-done.2
  428.4 2.4 collective-permute-done.3
  430.8 1.7 select_maximum_fusion
  432.5 0.9 fusion.21
  433.4 1.0 fusion.22
  434.4 0.9 fusion.23
  435.3 1.0 fusion.24
  436.4 0.9 fusion.29
  437.2 0.9 fusion.26
  438.1 0.9 fusion.18
  439.4 0.8 copy-done.10
  440.3 3.8 fusion.10
  (67 shorter events, 5.8 us)
Async XLA Ops:
  6.5 152.0 %copy-start = (bf16[1280,320]{0,1:T(8,128)(2,1)S(1)}, bf16[1280,320]{0,1:T(8,128)(2,1)}, u32[]{:S(2)}) copy-start(bf16[1280,320]{0,1:T(8,128)(2,1)} %param.17) | copy-start | bytes 2457604
  6.5 12.7 %copy-start.6 = (bf16[1,4,512,320]{2,3,1,0:T(8,128)(2,1)S(1)}, bf16[1,4,512,320]{2,3,1,0:T(8,128)(2,1)}, u32[]{:S(2)}) copy-start(bf16[1,4,512,320]{2,3,1,0:T(8,128)(2,1)} %param.9) | copy-start | bytes 3932164
  6.5 176.5 %all-gather.2.cloned.1.call-start = ((), (), s32[]{:S(2)}) async-start(), calls=%async_computation.1 | async-start | bytes 7520256 | tf_op jit(solution)/shard_map/all_gather | solution.py:111
  9.0 184.1 %all-to-all-start = ((bf16[16,1,64,320]{3,2,1,0:T(8,128)(2,1)}), bf16[16,1,64,320]{3,2,1,0:T(8,128)(2,1)}, u32[]{:S(2)}, u32[]{:S(2)}) async-start(bf16[16,1,64,320]{3,2,1,0:T(8,128)(2,1)} %stack.2), calls=%async_computation | async-start | bytes 1572864 | tf_op jit(solution)/shard_map/all_to_all | solution.py:113
  19.2 303.7 %all-reduce.4.cloned.1.call-start = ((), (), s32[]{:S(2)}) async-start(), calls=%async_computation.2 | async-start | bytes 884736 | tf_op jit(solution)/shard_map/psum | solution.py:119
  114.4 42.7 %copy-start.15 = (s32[256]{0:T(256)S(1)}, s32[256]{0:T(256)}, u32[]{:S(2)}) copy-start(s32[256]{0:T(256)} %param.12) | copy-start | bytes 3076
  114.4 44.1 %copy-start.14 = (bf16[1,1280]{1,0:T(2,128)(2,1)S(1)}, bf16[1,1280]{1,0:T(2,128)(2,1)}, u32[]{:S(2)}) copy-start(bf16[1,1280]{1,0:T(2,128)(2,1)} %param.10) | copy-start | bytes 7684
  149.9 12.3 %copy-start.2 = (bf16[1,4,512,320]{2,3,1,0:T(8,128)(2,1)}, bf16[1,4,512,320]{2,3,1,0:T(8,128)(2,1)S(1)}, u32[]{:S(2)}) copy-start(bf16[1,4,512,320]{2,3,1,0:T(8,128)(2,1)S(1)} %fusion.8) | copy-start | bytes 3932164
  150.0 12.3 %collective-permute-start = (bf16[1,1,512,320]{2,3,1,0:T(8,128)(2,1)S(1)}, bf16[1,1,512,320]{2,3,1,0:T(8,128)(2,1)S(1)}, u32[]{:S(2)}, u32[]{:S(2)}) collective-permute-start(bf16[1,1,512,320]{2,3,1,0:T(8,128)(2,1)S(1)} %get-tuple-element.7), channel_id=1, source_target_pairs={{0,16},{16,32},{32,48},{48,64},{64,80},{80,96},{96,112},{112,128},... | collective-permute-start | bytes 983048 | tf_op jit(solution)/shard_map/ppermute | solution.py:16
  152.2 10.8 %collective-permute-start.1 = (bf16[1,1,512,320]{2,3,1,0:T(8,128)(2,1)S(1)}, bf16[1,1,512,320]{2,3,1,0:T(8,128)(2,1)}, u32[]{:S(2)}, u32[]{:S(2)}) collective-permute-start(bf16[1,1,512,320]{2,3,1,0:T(8,128)(2,1)S(1)} %get-tuple-element.8), channel_id=1, source_target_pairs={{16,0},{32,16},{48,32},{64,48},{80,64},{96,80},{112,96},{128,112},... | collective-permute-start | bytes 983048 | tf_op jit(solution)/shard_map/ppermute | solution.py:17
  162.3 3.7 copy-start.11
  162.3 0.7 copy-start.8
  178.3 2.4 copy-start.3
  178.3 2.4 copy-start.9
  322.9 4.4 copy-start.4
  322.9 4.4 copy-start.13
  344.8 73.2 %copy-start.5 = (f32[4,512,320]{1,2,0:T(8,128)S(1)}, f32[4,512,320]{1,2,0:T(8,128)}, u32[]{:S(2)}) copy-start(f32[4,512,320]{1,2,0:T(8,128)} %get-tuple-element.10) | copy-start | bytes 7864324
  418.0 5.6 %copy-start.12 = (bf16[3,3,320,320]{3,2,1,0:T(8,128)(2,1)S(1)}, bf16[3,3,320,320]{3,2,1,0:T(8,128)(2,1)}, u32[]{:S(2)}) copy-start(bf16[3,3,320,320]{3,2,1,0:T(8,128)(2,1)} %param.16) | copy-start | bytes 5529604
  419.0 9.4 %collective-permute-start.2 = (bf16[1,1,512,320]{2,3,1,0:T(8,128)(2,1)S(1)}, bf16[1,1,512,320]{2,3,1,0:T(8,128)(2,1)S(1)}, u32[]{:S(2)}, u32[]{:S(2)}) collective-permute-start(bf16[1,1,512,320]{2,3,1,0:T(8,128)(2,1)S(1)} %get-tuple-element.5), channel_id=1, source_target_pairs={{0,16},{16,32},{32,48},{48,64},{64,80},{80,96},{96,112},{112,128},... | collective-permute-start | bytes 983048 | tf_op jit(solution)/shard_map/ppermute | solution.py:16
  420.9 9.9 %collective-permute-start.3 = (bf16[1,1,512,320]{2,3,1,0:T(8,128)(2,1)S(1)}, bf16[1,1,512,320]{2,3,1,0:T(8,128)(2,1)S(1)}, u32[]{:S(2)}, u32[]{:S(2)}) collective-permute-start(bf16[1,1,512,320]{2,3,1,0:T(8,128)(2,1)S(1)} %get-tuple-element.6), channel_id=1, source_target_pairs={{16,0},{32,16},{48,32},{64,48},{80,64},{96,80},{112,96},{128,112},... | collective-permute-start | bytes 983048 | tf_op jit(solution)/shard_map/ppermute | solution.py:17
  438.1 1.3 copy-start.7
  438.1 2.1 copy-start.10
  440.2 3.8 copy-start.1
Sparse Core Ops, SparseCore 0:
  9.1 103.7 all-gather.1
  189.5 133.4 all-reduce.3
